TPU v7x, 256 devices: a whole 4x4x8 slice. The times are simulated.
256 devices in a mesh: sec: 2 (over x_hi), gy: 16 (over y, x_lo, core), gz: 8 (over z).
Axes of the slice: x: 4 (x_hi: 2, x_lo: 2; x = x_hi * 2 + x_lo), y: 4, z: 8, core: 2. Of those that a mesh axis runs over, the one named last changes fastest.
Arguments:
- populations: float32 [56, 4, 128, 1024], P('sec', None, 'gy', 'gz'), may hold values from 0 to 1, as said below
- solid_mask: int32 [4, 128, 1024], P(None, 'gy', 'gz'), may hold values 0 or 1
- flow_rates: float32 [15], replicated, may hold values from 0.5 to 1.8
- species_rates: float32 [4], replicated, may hold values from 0.5 to 1.8
- cotangents: float32 [56, 4, 128, 1024], P('sec', None, 'gy', 'gz'), may hold values from -6 to 6
Outputs:
- next_pop: float32 [56, 4, 128, 1024], P('sec', None, 'gy', 'gz')
- pop_grad: float32 [56, 4, 128, 1024], P('sec', None, 'gy', 'gz')
- rate_grad: float32 [19], replicated
Inputs may be any that keep to these rules, and one draw needn't show every extreme that they name: `populations`: entries are positive.
All inputs are finite; a program needn't handle non-finite values. No bound on the sum of `solid_mask` on one device may be relied on, other than what follows from the above.
Results may differ from a plain program's by a relative error of at most 0.0003.
Values sent between devices are 32-bit elements; how exact they have to be, the bound alone decides.
No kernel may reach another device: no remote copies, remote signals or barrier semaphores. Data moves between devices by JAX's collectives and lax.ppermute only.
A program may use at most 64 MiB of HBM per device.

v0:
```python
from functools import partial
import jax
import jax.numpy as jnp
import numpy as np
from jax import lax
from jax.sharding import PartitionSpec as P


def extended(block, sides, width):
    for axis, dim in sides:
        count = lax.axis_size(axis)
        forward = [(i, i + 1) for i in range(count - 1)]
        forward.append((count - 1, 0))
        backward = [(target, source) for source, target in forward]
        low = lax.ppermute(
            lax.slice_in_dim(block, block.shape[dim] - width, None, axis=dim), axis, forward
        )
        high = lax.ppermute(lax.slice_in_dim(block, 0, width, axis=dim), axis, backward)
        block = jnp.concatenate([low, block, high], axis=dim)
    return block


def spread(shard, axis, root):
    mine = lax.axis_index(axis) == root
    return lax.psum(jnp.where(mine, shard, jnp.zeros_like(shard)), axis)


def orthonormal_columns(basis):
    result = []
    for column in range(basis.shape[1]):
        vector = basis[:, column] * 1.0
        for repeat in range(2):
            for earlier in result:
                vector = vector - np.sum(earlier * vector) * earlier
        vector = vector / np.sqrt(np.sum(vector * vector))
        result.append(vector)
    return np.stack(result, 1)


def lattice_tables():
    axis_moves = [(1, 0, 0), (-1, 0, 0), (0, 1, 0), (0, -1, 0), (0, 0, 1), (0, 0, -1)]
    edge_moves = []
    for first, second in ((0, 1), (0, 2), (1, 2)):
        for sign_first in (1, -1):
            for sign_second in (1, -1):
                move = [0, 0, 0]
                move[first] = sign_first
                move[second] = sign_second
                edge_moves.append(tuple(move))
    velocity = np.array([(0, 0, 0)] + axis_moves + edge_moves) * 1.0
    weights = np.array([1.0 / 3.0] + [1.0 / 18.0] * 6 + [1.0 / 36.0] * 12)
    opposite = np.array(
        [int(np.argmin(np.abs(velocity + velocity[channel]).sum(1))) for channel in range(19)]
    )
    along_x = velocity[:, 0]
    along_y = velocity[:, 1]
    along_z = velocity[:, 2]
    basis = np.stack(
        [
            np.ones(19),
            along_x,
            along_y,
            along_z,
            along_x**2,
            along_y**2,
            along_z**2,
            along_x * along_y,
            along_y * along_z,
            along_x * along_z,
            along_x * along_y**2,
            along_x * along_z**2,
            along_y * along_x**2,
            along_y * along_z**2,
            along_z * along_x**2,
            along_z * along_y**2,
            along_x**2 * along_y**2,
            along_x**2 * along_z**2,
            along_y**2 * along_z**2,
        ],
        1,
    )
    ortho = orthonormal_columns(basis)
    return (velocity, weights, opposite, ortho)


def expand(table, trailing):
    return jnp.asarray(table, jnp.float32).reshape(table.shape + (1,) * trailing)


def same_move(first_move, second_move):
    return tuple((int(value) for value in first_move)) == tuple(
        (int(value) for value in second_move)
    )


def flow_branch(is_fluid, rows, motion, flow_rates, species_rates):
    velocity, weights, opposite, ortho = lattice_tables()
    highest = lax.Precision.HIGHEST
    flow = rows[:19]
    trailing = flow.ndim - 1
    rates = jnp.concatenate([jnp.zeros((4,), flow_rates.dtype), flow_rates])
    ortho_table = jnp.asarray(ortho, jnp.float32)
    collision = jnp.dot(ortho_table * rates[None, :], ortho_table.T, precision=highest)
    velocity_table = jnp.asarray(velocity, jnp.float32)
    density = jnp.sum(flow, 0)
    projected = jnp.tensordot(velocity_table, motion, 1, precision=highest)
    squared = jnp.sum(motion * motion, 0)
    equilibrium = (
        expand(weights, trailing)
        * density
        * (1.0 + 3.0 * projected + 4.5 * projected * projected - 1.5 * squared)
    )
    relaxed = flow - jnp.tensordot(collision, flow - equilibrium, 1, precision=highest)
    flow_out = jnp.where(is_fluid, relaxed, flow[opposite])
    filler = jnp.zeros((rows.shape[0] - 19,) + rows.shape[1:], jnp.float32)
    return jnp.concatenate([flow_out, filler])


def species_branch(is_fluid, rows, motion, flow_rates, species_rates):
    velocity, weights, opposite, ortho = lattice_tables()
    highest = lax.Precision.HIGHEST
    trailing = rows.ndim - 1
    velocity_table = jnp.asarray(velocity[:7], jnp.float32)
    projected = jnp.tensordot(velocity_table, motion, 1, precision=highest)
    grouped = rows.reshape((rows.shape[0] // 7, 7) + rows.shape[1:])
    concentration = jnp.sum(grouped, 1)
    small_weights = np.array([0.25] + [0.125] * 6)
    species_eq = (
        expand(small_weights, trailing)[None]
        * concentration[:, None]
        * (1.0 + 4.0 * projected)[None]
    )
    rate_shape = species_rates.reshape((-1, 1) + (1,) * trailing)
    relaxed_species = grouped - rate_shape * (grouped - species_eq)
    return jnp.where(is_fluid, relaxed_species, grouped[:, opposite[:7]]).reshape(rows.shape)


def take_piece(padded, channel, move, size_y, size_z):
    step_x, step_y, step_z = (int(value) for value in move)
    piece = padded[channel, :, 1 - step_y : 1 - step_y + size_y, 1 - step_z : 1 - step_z + size_z]
    return jnp.roll(piece, step_x, 0)


def stream(field, table_flow, table_species, is_flow):
    padded = extended(field, (("gy", 2), ("gz", 3)), 1)
    size_y, size_z = (field.shape[2], field.shape[3])
    pieces = []
    for channel in range(field.shape[0]):
        first = take_piece(padded, channel, table_flow[channel], size_y, size_z)
        if same_move(table_flow[channel], table_species[channel]):
            pieces.append(first)
        else:
            second = take_piece(padded, channel, table_species[channel], size_y, size_z)
            pieces.append(jnp.where(is_flow, first, second))
    return jnp.stack(pieces)


def per_device(populations, solid_mask, flow_rates, species_rates, cotangents):
    velocity, weights, opposite, ortho = lattice_tables()
    highest = lax.Precision.HIGHEST
    rows_count = populations.shape[0]
    is_flow = lax.axis_index("sec") == 0
    is_fluid = solid_mask == 0
    velocity_table = jnp.asarray(velocity, jnp.float32)
    density = jnp.sum(populations[:19], 0)
    own_motion = jnp.tensordot(velocity_table.T, populations[:19], 1, precision=highest) / density
    motion = spread(own_motion, "sec", 0)

    def forward(rows, shared, rates_a, rates_b):
        return lax.cond(
            is_flow,
            partial(flow_branch, is_fluid),
            partial(species_branch, is_fluid),
            rows,
            shared,
            rates_a,
            rates_b,
        )

    post, pullback = jax.vjp(forward, populations, motion, flow_rates, species_rates)
    table_flow = np.concatenate([velocity, np.zeros((rows_count - 19, 3))])
    table_species = np.tile(velocity[:7], (rows_count // 7, 1))
    returned = stream(cotangents, -table_flow, -table_species, is_flow)
    moved = stream(post, table_flow, table_species, is_flow)
    grad_rows, grad_motion, local_flow_rates, local_species_rates = pullback(returned)
    from_species = spread(grad_motion, "sec", 1)
    total_motion = grad_motion + from_species
    along = jnp.tensordot(velocity_table, total_motion, 1, precision=highest)
    extra = (along - jnp.sum(own_motion * total_motion, 0)[None]) / density[None]
    filler = jnp.zeros((rows_count - 19,) + populations.shape[1:], jnp.float32)
    grad_rows = grad_rows + jnp.where(is_flow, jnp.concatenate([extra, filler]), 0.0)
    summed_flow_rates, summed_species_rates = lax.psum(
        (local_flow_rates, local_species_rates), ("sec", "gy", "gz")
    )
    rate_grad = jnp.concatenate([summed_flow_rates, summed_species_rates])
    return (moved, grad_rows, rate_grad)


def solution(mesh):
    placed = (P("sec", None, "gy", "gz"), P(None, "gy", "gz"), P(), P(), P("sec", None, "gy", "gz"))
    return jax.shard_map(
        per_device,
        mesh=mesh,
        in_specs=placed,
        out_specs=(P("sec", None, "gy", "gz"), P("sec", None, "gy", "gz"), P()),
        check_vma=False,
    )
```

profile of v0, /device:TPU:1, one launch (start us, length us, event | category | flops | bytes accessed | tf_op | source)
XLA Modules:
  0.0 205.7 jit_solution(12356524541416200816)
XLA Ops:
  0.6 0.7 broadcast_compare_fusion
  1.4 1.0 slice_reduce_fusion.1
  2.4 1.1 broadcast_select_fusion.4
  3.5 10.7 %psum.28 = f32[3,4,8,128]{3,0,2,1:T(4,128)S(1)} all-reduce(f32[3,4,8,128]{3,0,2,1:T(4,128)S(1)} %get-tuple-element.572), channel_id=1, replica_groups=mesh['sec'=2,'gy'=16,'gz'=8] {'sec'}, use_global_device_ids=true, to_apply=%region_1.2 | all-reduce | flops 12288 | bytes 98304 | tf_op jit(solution)/shard_map/psum | solution.py:25
  14.9 8.5 %conditional.2 = (f32[28,4,8,128]{3,0,2,1:T(8,128)S(1)}, f32[7,3]{1,0:T(8,128)S(1)}, f32[1,7,1,1,1]{4,3,2,1,0:T(1,128)S(1)}, f32[1,7,4,8,128]{4,3,2,1,0:T(8,128)...) conditional(s32[]{:T(128)} %convert_element_type.3, ...), branch_computations={%region_2.4_spmd.clone, %region_4.7_spmd.clone} | conditional | flops 21583616 | bytes 10085426 | solution.py:170
  16.0 1.6 multiply_subtract_fusion.1
  21.1 0.7 copy-done.68
  28.3 2.9 %collective-permute-start = (f32[28,4,1,128]{3,2,1,0:T(1,128)}, f32[28,4,1,128]{3,2,1,0:T(1,128)S(1)}, u32[]{:S(2)}, u32[]{:S(2)}) collective-permute-start(f32[28,4,1,128]{3,2,1,0:T(1,128)} %copy.353), channel_id=1, source_target_pairs={{0,8},{8,16},{16,24},{24,32},{32,40},{40,48},{48,56},{56,64},{64,7... | collective-permute-start | bytes 172040 | tf_op jit(solution)/shard_map/ppermute | solution.py:15
  31.8 0.7 fusion.71
  32.6 3.8 %collective-permute-start.4 = (f32[28,4,1,128]{3,2,1,0:T(1,128)}, f32[28,4,1,128]{3,2,1,0:T(1,128)S(1)}, u32[]{:S(2)}, u32[]{:S(2)}) collective-permute-start(f32[28,4,1,128]{3,2,1,0:T(1,128)} %get-tuple-element.553), channel_id=1, source_target_pairs={{8,0},{16,8},{24,16},{32,24},{40,32},{48,40},{56,48},{64,56},{72,6... | collective-permute-start | bytes 172040 | tf_op jit(solution)/shard_map/ppermute | solution.py:18
  36.4 1.1 constant_dynamic-update-slice_fusion
  40.6 0.8 constant_dynamic-update-slice_fusion.29
  42.6 2.8 %dynamic-update-slice.59 = f32[28,4,9,128]{3,2,1,0:T(8,128)} dynamic-update-slice(f32[28,4,9,128]{3,2,1,0:T(8,128)} %get-tuple-element.508, f32[28,4,1,128]{3,2,1,0:T(1,128)S(1)} %collective-permute-done.1, s32[]{} %constant.121, s32[]{} %constant.121, s32[]{} %constant.129, s32[]{} %constant.121) | dynamic-update-slice | bytes 114692 | tf_op jit(solution)/shard_map/concatenate | solution.py:19
  45.4 1.4 fusion.65
  47.4 1.4 constant_dynamic-update-slice_fusion.24
  49.3 1.3 fusion.66
  50.6 2.8 %dynamic-update-slice.29 = f32[28,4,9,128]{3,2,1,0:T(8,128)} dynamic-update-slice(f32[28,4,9,128]{3,2,1,0:T(8,128)} %constant_dynamic-update-slice_fusion.29, f32[28,4,1,128]{3,2,1,0:T(1,128)S(1)} %collective-permute-done.4, s32[]{} %constant.121, s32[]{} %constant.121, s32[]{} %constant.129, s32[]{} %constant.121) | dynamic-update-slice | bytes 114692 | tf_op jit(solution)/shard_map/concatenate | solution.py:19
  53.4 1.4 fusion.63
  54.7 0.8 constant_dynamic-update-slice_fusion.54
  55.5 1.3 fusion.62
  56.8 1.3 copy.358
  58.0 1.5 collective-permute-start.2
  59.5 1.3 copy.360
  60.8 3.9 %collective-permute-start.3 = (f32[28,4,10,1]{0,2,3,1:T(8,128)}, f32[28,4,10,1]{0,2,3,1:T(8,128)}, u32[]{:S(2)}, u32[]{:S(2)}) collective-permute-start(f32[28,4,10,1]{0,2,3,1:T(8,128)} %copy.360), channel_id=1, source_target_pairs={{1,0},{2,1},{3,2},{4,3},{5,4},{6,5},{7,6},{0,7},{9,8},{10,9},{11,1... | collective-permute-start | bytes 13448 | tf_op jit(solution)/shard_map/ppermute | solution.py:18
  65.2 1.3 copy.385
  66.5 1.5 collective-permute-start.6
  68.0 1.3 copy.387
  69.2 1.7 copy.359
  70.9 1.7 copy.361
  77.3 1.4 constant_dynamic-update-slice_fusion.17
  83.0 1.4 constant_dynamic-update-slice_fusion.10
  88.4 1.4 constant_dynamic-update-slice_fusion.3
  89.8 2.5 %copy.386 = f32[28,4,10,1]{3,2,1,0:T(8,128)} copy(f32[28,4,10,1]{0,2,3,1:T(8,128)} %collective-permute-done.6) | data formatting | bytes 8960 | tf_op jit(solution)/shard_map/ppermute | solution.py:18
  92.3 2.5 %copy.388 = f32[28,4,10,1]{3,2,1,0:T(8,128)} copy(f32[28,4,10,1]{0,2,3,1:T(8,128)} %collective-permute-done.7) | data formatting | bytes 8960 | tf_op jit(solution)/shard_map/ppermute | solution.py:15
  94.8 0.9 constant_dynamic-update-slice_fusion.52
  96.8 0.8 constant_dynamic-update-slice_fusion.47
  99.4 0.8 constant_dynamic-update-slice_fusion.40
  101.8 0.8 constant_dynamic-update-slice_fusion.33
  103.5 9.2 %conditional.3 = (f32[3,4,8,128]{3,0,2,1:T(4,128)S(1)}, f32[15]{0:T(128)S(1)}, f32[4]{0:T(128)S(1)}, f32[28,4,8,128]{3,0,2,1:T(8,128)}) conditional(s32[]{:T(128)} %convert_element_type.3, (f32[28,4,8,128]{3,2,1,0:T(8,128)S(1)}, pred[4,7,4,8,128]{4,3,2,1,0:T(8,128)(4,1)}, f32[4,1,1,1,1]{4,3,2,1,0:T(1,128)S(1)}, f32[1,7,1,1,1]{4,3,2,1,0:T(1,128)}, ...), branch_computations={%region_7.12_spmd, %region_12.17_spmd} | conditional | flops 40199236 | bytes 13603772 | solution.py:170
  103.9 0.7 copy-done.7
  104.6 1.7 multiply_reduce_fusion.4
  106.4 1.5 fusion.15
  109.7 1.9 scatter_fusion.1
  111.8 0.9 pad.5.clone
  113.3 8.1 %psum.29 = f32[3,4,8,128]{3,0,2,1:T(4,128)S(1)} all-reduce(f32[3,4,8,128]{3,0,2,1:T(4,128)S(1)} %broadcast_select_fusion.3), channel_id=1, replica_groups=mesh['sec'=2,'gy'=16,'gz'=8] {'sec'}, use_global_device_ids=true, to_apply=%region_17.18 | all-reduce | flops 12288 | bytes 98304 | tf_op jit(solution)/shard_map/psum | solution.py:25
  122.6 1.1 select_add_fusion
  123.7 1.0 copy.398
  125.4 78.3 %all-reduce.4 = (f32[4]{0:T(128)S(1)}, f32[15]{0:T(128)S(1)}) all-reduce(f32[4]{0:T(128)S(1)} %get-tuple-element.174, f32[15]{0:T(128)S(1)} %copy-done.85), channel_id=1, replica_groups=mesh['sec'=2,'gy'=16,'gz'=8] {'sec','gy','gz'}, use_global_device_ids=true, to_apply=%region_20.21 | all-reduce | flops 19 | bytes 152 | tf_op jit(solution)/shard_map/psum | solution.py:192
  (264 shorter events, 42.9 us)
Async XLA Ops:
  1.4 1.0 copy-start.86
  2.4 1.2 copy-start.49
  2.4 11.9 %copy-start.3 = (f32[28,4,8,128]{3,2,1,0:T(8,128)S(1)}, f32[28,4,8,128]{3,2,1,0:T(8,128)}, u32[]{:S(2)}) copy-start(f32[28,4,8,128]{3,2,1,0:T(8,128)} %param.19) | copy-start | bytes 1376260
  14.9 4.4 %copy-start.8 = (pred[19,4,8,128]{3,0,2,1:T(8,128)(4,1)}, pred[19,4,8,128]{3,0,2,1:T(8,128)(4,1)S(1)}, u32[]{:S(2)}) copy-start(pred[19,4,8,128]{3,0,2,1:T(8,128)(4,1)S(1)} %broadcast_in_dim.48) | copy-start | bytes 233476 | tf_op jit(solution)/shard_map/jvp()/cond
  17.6 1.8 copy-start.4
  17.7 0.8 copy-start.80
  21.1 0.7 copy-start.68
  22.5 0.9 copy-start.9
  22.6 0.9 copy-start.17
  27.0 4.8 %copy-start.12 = (f32[3,4,8,128]{3,0,2,1:T(4,128)}, f32[3,4,8,128]{3,0,2,1:T(4,128)S(1)}, u32[]{:S(2)}) copy-start(f32[3,4,8,128]{3,0,2,1:T(4,128)S(1)} %get-tuple-element.164) | copy-start | bytes 147460
  27.0 10.5 %copy-start.6 = (f32[19,4,8,128]{3,0,2,1:T(8,128)}, f32[19,4,8,128]{3,0,2,1:T(8,128)S(1)}, u32[]{:S(2)}) copy-start(f32[19,4,8,128]{3,0,2,1:T(8,128)S(1)} %get-tuple-element.163) | copy-start | bytes 933892
  27.0 10.5 %copy-start.10 = (f32[4,7,4,8,128]{4,3,2,1,0:T(8,128)}, f32[4,7,4,8,128]{4,3,2,1,0:T(8,128)S(1)}, u32[]{:S(2)}) copy-start(f32[4,7,4,8,128]{4,3,2,1,0:T(8,128)S(1)} %get-tuple-element.157) | copy-start | bytes 1376260
  27.0 10.5 %copy-start.11 = (f32[4,7,4,8,128]{4,3,2,1,0:T(8,128)}, f32[4,7,4,8,128]{4,3,2,1,0:T(8,128)S(1)}, u32[]{:S(2)}) copy-start(f32[4,7,4,8,128]{4,3,2,1,0:T(8,128)S(1)} %get-tuple-element.155) | copy-start | bytes 1376260
  27.0 10.4 %copy-start.14 = (f32[19,4,8,128]{3,0,2,1:T(8,128)}, f32[19,4,8,128]{3,0,2,1:T(8,128)S(1)}, u32[]{:S(2)}) copy-start(f32[19,4,8,128]{3,0,2,1:T(8,128)S(1)} %get-tuple-element.166) | copy-start | bytes 933892
  27.0 4.8 %copy-start = (f32[28,4,8,128]{3,2,1,0:T(8,128)S(1)}, f32[28,4,8,128]{3,2,1,0:T(8,128)}, u32[]{:S(2)}) copy-start(f32[28,4,8,128]{3,2,1,0:T(8,128)} %param.23) | copy-start | bytes 1376260
  28.3 18.5 %collective-permute-start = (f32[28,4,1,128]{3,2,1,0:T(1,128)}, f32[28,4,1,128]{3,2,1,0:T(1,128)S(1)}, u32[]{:S(2)}, u32[]{:S(2)}) collective-permute-start(f32[28,4,1,128]{3,2,1,0:T(1,128)} %copy.353), channel_id=1, source_target_pairs={{0,8},{8,16},{16,24},{24,32},{32,40},{40,48},{48,56},{56,64},{64,7... | collective-permute-start | bytes 172040 | tf_op jit(solution)/shard_map/ppermute | solution.py:15
  31.8 10.8 %collective-permute-start.1 = (f32[28,4,1,128]{3,2,1,0:T(1,128)}, f32[28,4,1,128]{3,2,1,0:T(1,128)S(1)}, u32[]{:S(2)}, u32[]{:S(2)}) collective-permute-start(f32[28,4,1,128]{3,2,1,0:T(1,128)} %copy.355), channel_id=1, source_target_pairs={{8,0},{16,8},{24,16},{32,24},{40,32},{48,40},{56,48},{64,56},{72,6... | collective-permute-start | bytes 172040 | tf_op jit(solution)/shard_map/ppermute | solution.py:18
  32.6 18.0 %collective-permute-start.4 = (f32[28,4,1,128]{3,2,1,0:T(1,128)}, f32[28,4,1,128]{3,2,1,0:T(1,128)S(1)}, u32[]{:S(2)}, u32[]{:S(2)}) collective-permute-start(f32[28,4,1,128]{3,2,1,0:T(1,128)} %get-tuple-element.553), channel_id=1, source_target_pairs={{8,0},{16,8},{24,16},{32,24},{40,32},{48,40},{56,48},{64,56},{72,6... | collective-permute-start | bytes 172040 | tf_op jit(solution)/shard_map/ppermute | solution.py:18
  36.4 28.4 %collective-permute-start.5 = (f32[28,4,1,128]{3,2,1,0:T(1,128)}, f32[28,4,1,128]{3,2,1,0:T(1,128)S(1)}, u32[]{:S(2)}, u32[]{:S(2)}) collective-permute-start(f32[28,4,1,128]{3,2,1,0:T(1,128)} %get-tuple-element.552), channel_id=1, source_target_pairs={{0,8},{8,16},{16,24},{24,32},{32,40},{40,48},{48,56},{56,64},{64,7... | collective-permute-start | bytes 172040 | tf_op jit(solution)/shard_map/ppermute | solution.py:15
  58.0 11.2 %collective-permute-start.2 = (f32[28,4,10,1]{0,2,3,1:T(8,128)}, f32[28,4,10,1]{0,2,3,1:T(8,128)}, u32[]{:S(2)}, u32[]{:S(2)}) collective-permute-start(f32[28,4,10,1]{0,2,3,1:T(8,128)} %copy.358), channel_id=1, source_target_pairs={{0,1},{1,2},{2,3},{3,4},{4,5},{5,6},{6,7},{7,0},{8,9},{9,10},{10,1... | collective-permute-start | bytes 13448 | tf_op jit(solution)/shard_map/ppermute | solution.py:15
  60.8 10.1 %collective-permute-start.3 = (f32[28,4,10,1]{0,2,3,1:T(8,128)}, f32[28,4,10,1]{0,2,3,1:T(8,128)}, u32[]{:S(2)}, u32[]{:S(2)}) collective-permute-start(f32[28,4,10,1]{0,2,3,1:T(8,128)} %copy.360), channel_id=1, source_target_pairs={{1,0},{2,1},{3,2},{4,3},{5,4},{6,5},{7,6},{0,7},{9,8},{10,9},{11,1... | collective-permute-start | bytes 13448 | tf_op jit(solution)/shard_map/ppermute | solution.py:18
  66.5 23.3 %collective-permute-start.6 = (f32[28,4,10,1]{0,2,3,1:T(8,128)}, f32[28,4,10,1]{0,2,3,1:T(8,128)}, u32[]{:S(2)}, u32[]{:S(2)}) collective-permute-start(f32[28,4,10,1]{0,2,3,1:T(8,128)} %copy.385), channel_id=1, source_target_pairs={{1,0},{2,1},{3,2},{4,3},{5,4},{6,5},{7,6},{0,7},{9,8},{10,9},{11,1... | collective-permute-start | bytes 13448 | tf_op jit(solution)/shard_map/ppermute | solution.py:18
  69.2 23.1 %collective-permute-start.7 = (f32[28,4,10,1]{0,2,3,1:T(8,128)}, f32[28,4,10,1]{0,2,3,1:T(8,128)}, u32[]{:S(2)}, u32[]{:S(2)}) collective-permute-start(f32[28,4,10,1]{0,2,3,1:T(8,128)} %copy.387), channel_id=1, source_target_pairs={{0,1},{1,2},{2,3},{3,4},{4,5},{5,6},{6,7},{7,0},{8,9},{9,10},{10,1... | collective-permute-start | bytes 13448 | tf_op jit(solution)/shard_map/ppermute | solution.py:15
  74.0 0.7 copy-start.35
  74.0 0.7 copy-start.63
  75.3 0.7 copy-start.37
  75.3 0.7 copy-start.47
  85.1 2.0 copy-start.28
  85.8 0.7 copy-start.55
  94.8 1.2 copy-start.2
  96.0 0.7 copy-start.36
  96.0 0.7 copy-start.44
  96.0 0.7 copy-start.27
  96.0 0.7 copy-start.33
  96.0 0.7 copy-start.53
  96.0 0.7 copy-start.61
  96.1 1.4 copy-start.1
  100.4 0.8 copy-start.25
  100.4 0.7 copy-start.26
  100.4 0.7 copy-start.52
  102.8 0.7 copy-start.19
  102.8 0.7 copy-start.40
  103.6 1.0 copy-start.7
  104.6 1.7 copy-start.13
  104.6 1.8 copy-start.15
  106.4 1.6 copy-start.5
  113.2 8.1 %copy-start.20 = (f32[3,4,8,128]{3,0,2,1:T(4,128)S(1)}, f32[3,4,8,128]{3,0,2,1:T(4,128)}, u32[]{:S(2)}) copy-start(f32[3,4,8,128]{3,0,2,1:T(4,128)} %get-tuple-element.573) | copy-start | bytes 147460
  121.4 0.7 copy-start.50
  (39 other events, 26.1 us)
where the time goes:
time: 208 us; the launch traced here: 206 us
  blocking collectives  97.1 us (47%)
  local copies, waits for them, and re-layouts  56.7 us (27%)
  other arithmetic  29 us (14%)
  starting transfers between devices  13.6 us (7%)
  matrix products  7.89 us (4%)
    psum x1, blocking collectives, per_device(): lax.psum((local_flow_rates, local_species_rates), ('sec', 'gy', 'gz'))  78.3 us
    unnamed x48, other arithmetic  22.2 us
    psum x2, blocking collectives, spread(): return lax.psum(jnp.where(mine, shard, jnp.zeros_like(shard)), axis)  18.8 us
    unnamed x131, local copies, waits for them, and re-layouts  18.2 us
    ppermute x4, starting transfers between devices, extended(): lax.ppermute(lax.slice_in_dim(block, 0, width, axis=dim), axis, backward)  9.2 us
    slice x8, local copies, waits for them, and re-layouts, take_piece(): return jnp.roll(piece, step_x, 0)  7.86 us
    concatenate x2, local copies, waits for them, and re-layouts, extended(): block = jnp.concatenate([low, block, high], axis=dim)  5.54 us
    cond x40, local copies, waits for them, and re-layouts  5.1 us
  transfers between devices with their start and end apart: 8, of which 0 were waited for; matrix products, arithmetic and copies ran while one was open for 24% of the time, Pallas kernels for 0%

commit v1 on v0

--- a/solution.py
+++ b/solution.py
@@ -190,7 +190,7 @@
     filler = jnp.zeros((rows_count - 19,) + populations.shape[1:], jnp.float32)
     grad_rows = grad_rows + jnp.where(is_flow, jnp.concatenate([extra, filler]), 0.0)
     summed_flow_rates, summed_species_rates = lax.psum(
-        (local_flow_rates, local_species_rates), ("sec", "gy", "gz")
+        lax.psum((local_flow_rates, local_species_rates), "sec"), ("gy", "gz")
     )
     rate_grad = jnp.concatenate([summed_flow_rates, summed_species_rates])
     return (moved, grad_rows, rate_grad)

time: 208 us -> 410 us (1.97)
  the two profiles are of different devices: /device:TPU:1 before, /device:TPU:4 now
where the time goes in v1:
time: 410 us; the launch traced here: 408 us
  blocking collectives  302 us (74%)
  local copies, waits for them, and re-layouts  59.5 us (15%)
  other arithmetic  31.9 us (8%)
  starting transfers between devices  10.8 us (3%)
    psum x1, blocking collectives, per_device(): lax.psum(lax.psum((local_flow_rates, local_species_rates), 'sec'), ('gy',...  279 us
    psum x2, blocking collectives, spread(): return lax.psum(jnp.where(mine, shard, jnp.zeros_like(shard)), axis)  22.9 us
    unnamed x48, other arithmetic  22.2 us
    unnamed x129, local copies, waits for them, and re-layouts  17.5 us
    ppermute x4, starting transfers between devices, extended(): lax.ppermute(lax.slice_in_dim(block, 0, width, axis=dim), axis, backward)  9.82 us
  transfers between devices with their start and end apart: 8, of which 0 were waited for; matrix products, arithmetic and copies ran while one was open for 12% of the time, Pallas kernels for 0%

profile of v1, /device:TPU:4, one launch (start us, length us, event | category | flops | bytes accessed | tf_op | source)
XLA Modules:
  0.0 408.1 jit_solution(9388792397319141078)
XLA Ops:
  0.6 0.7 broadcast_compare_fusion
  1.4 1.0 slice_reduce_fusion.1
  2.4 1.1 broadcast_select_fusion.4
  3.5 11.1 %psum.42 = f32[3,4,8,128]{3,0,2,1:T(4,128)S(1)} all-reduce(f32[3,4,8,128]{3,0,2,1:T(4,128)S(1)} %get-tuple-element.575), channel_id=1, replica_groups=mesh['sec'=2,'gy'=16,'gz'=8] {'sec'}, use_global_device_ids=true, to_apply=%region_1.2 | all-reduce | flops 12288 | bytes 98304 | tf_op jit(solution)/shard_map/psum | solution.py:25
  15.3 9.5 %conditional.2 = (f32[28,4,8,128]{3,0,2,1:T(8,128)S(1)}, f32[7,3]{1,0:T(8,128)S(1)}, f32[1,7,1,1,1]{4,3,2,1,0:T(1,128)S(1)}, f32[1,7,4,8,128]{4,3,2,1,0:T(8,128)...) conditional(s32[]{:T(128)} %convert_element_type.3, ...), branch_computations={%region_2.4_spmd.clone, %region_4.7_spmd.clone} | conditional | flops 21583616 | bytes 10085426 | solution.py:170
  21.8 0.8 broadcast.204.clone
  22.6 0.8 broadcast.204.clone.1
  23.4 0.8 broadcast.204.clone.3
  30.3 3.9 collective-permute-start.1
  34.2 0.7 fusion.71
  35.4 1.1 constant_dynamic-update-slice_fusion
  39.6 0.8 constant_dynamic-update-slice_fusion.29
  41.7 2.8 dynamic-update-slice.59
  44.5 1.4 fusion.65
  46.4 1.4 constant_dynamic-update-slice_fusion.24
  48.3 1.3 fusion.66
  49.6 2.8 dynamic-update-slice.29
  52.4 1.4 fusion.63
  53.7 0.8 constant_dynamic-update-slice_fusion.54
  54.5 1.3 fusion.62
  55.8 1.3 copy.358
  57.6 1.3 copy.360
  58.8 3.9 collective-permute-start.3
  63.3 1.3 copy.385
  64.5 2.0 collective-permute-start.6
  66.6 1.3 copy.387
  67.8 1.7 copy.359
  69.5 1.7 copy.361
  75.9 1.4 constant_dynamic-update-slice_fusion.17
  77.4 0.7 constant_dynamic-update-slice_fusion.16
  81.6 1.4 constant_dynamic-update-slice_fusion.10
  87.0 1.4 constant_dynamic-update-slice_fusion.3
  88.4 2.5 copy.386
  90.9 2.5 copy.388
  93.4 0.9 constant_dynamic-update-slice_fusion.52
  95.4 0.8 constant_dynamic-update-slice_fusion.47
  97.9 0.8 constant_dynamic-update-slice_fusion.40
  100.4 0.8 constant_dynamic-update-slice_fusion.33
  102.1 8.8 %conditional.3 = (f32[3,4,8,128]{3,0,2,1:T(4,128)S(1)}, f32[15]{0:T(128)S(1)}, f32[4]{0:T(128)S(1)}, f32[28,4,8,128]{3,0,2,1:T(8,128)}) conditional(s32[]{:T(128)} %convert_element_type.3, (f32[28,4,8,128]{3,2,1,0:T(8,128)S(1)}, pred[4,7,4,8,128]{4,3,2,1,0:T(8,128)(4,1)}, f32[4,1,1,1,1]{4,3,2,1,0:T(1,128)S(1)}, f32[1,7,1,1,1]{4,3,2,1,0:T(1,128)}, ...), branch_computations={%region_7.12_spmd, %region_12.17_spmd} | conditional | flops 40199236 | bytes 13603772 | solution.py:170
  103.0 1.5 multiply_reduce_fusion.3
  105.5 1.8 select_bitcast_fusion
  107.4 1.0 copy.342
  108.5 1.3 scatter_fusion
  109.8 1.1 copy.410
  111.5 11.8 %all-reduce.5 = (f32[3,4,8,128]{3,0,2,1:T(4,128)S(1)}, f32[4]{0:T(128)S(1)}, f32[15]{0:T(128)S(1)}) all-reduce(f32[3,4,8,128]{3,0,2,1:T(4,128)S(1)} %broadcast_select_fusion.3, f32[4]{0:T(128)S(1)} %get-tuple-element.174, f32[15]{0:T(128)} %copy-done.79), channel_id=1, replica_groups=mesh['sec'=2,'gy'=16,'gz'=8] {'sec'}, use_global_device_ids=true, to_apply=%region_17.18 | all-reduce | flops 12307 | bytes 98456 | tf_op jit(solution)/shard_map/psum | solution.py:25
  124.5 1.1 select_add_fusion
  125.6 1.0 copy.398
  126.7 279.5 %all-reduce.4 = (f32[4]{0:T(128)S(1)}, f32[15]{0:T(128)S(1)}) all-reduce(f32[4]{0:T(128)S(1)} %get-tuple-element.503, f32[15]{0:T(128)S(1)} %get-tuple-element.504), channel_id=1, replica_groups=mesh['sec'=2,'gy'=16,'gz'=8] {'gy','gz'}, use_global_device_ids=true, to_apply=%region_22.23 | all-reduce | flops 19 | bytes 152 | tf_op jit(solution)/shard_map/psum | solution.py:192
  (248 shorter events, 43.2 us)
Async XLA Ops:
  1.4 1.0 copy-start.85
  2.4 1.2 copy-start.49
  2.4 12.3 %copy-start.3 = (f32[28,4,8,128]{3,2,1,0:T(8,128)S(1)}, f32[28,4,8,128]{3,2,1,0:T(8,128)}, u32[]{:S(2)}) copy-start(f32[28,4,8,128]{3,2,1,0:T(8,128)} %param.19) | copy-start | bytes 1376260
  28.4 2.0 copy-start.12
  28.4 8.1 %copy-start.6 = (f32[19,4,8,128]{3,0,2,1:T(8,128)}, f32[19,4,8,128]{3,0,2,1:T(8,128)S(1)}, u32[]{:S(2)}) copy-start(f32[19,4,8,128]{3,0,2,1:T(8,128)S(1)} %get-tuple-element.163) | copy-start | bytes 933892
  28.4 8.1 %copy-start.10 = (f32[4,7,4,8,128]{4,3,2,1,0:T(8,128)}, f32[4,7,4,8,128]{4,3,2,1,0:T(8,128)S(1)}, u32[]{:S(2)}) copy-start(f32[4,7,4,8,128]{4,3,2,1,0:T(8,128)S(1)} %get-tuple-element.157) | copy-start | bytes 1376260
  28.4 8.1 %copy-start.11 = (f32[4,7,4,8,128]{4,3,2,1,0:T(8,128)}, f32[4,7,4,8,128]{4,3,2,1,0:T(8,128)S(1)}, u32[]{:S(2)}) copy-start(f32[4,7,4,8,128]{4,3,2,1,0:T(8,128)S(1)} %get-tuple-element.155) | copy-start | bytes 1376260
  28.4 8.1 %copy-start.14 = (f32[19,4,8,128]{3,0,2,1:T(8,128)}, f32[19,4,8,128]{3,0,2,1:T(8,128)S(1)}, u32[]{:S(2)}) copy-start(f32[19,4,8,128]{3,0,2,1:T(8,128)S(1)} %get-tuple-element.166) | copy-start | bytes 933892
  28.4 5.8 %copy-start = (f32[28,4,8,128]{3,2,1,0:T(8,128)S(1)}, f32[28,4,8,128]{3,2,1,0:T(8,128)}, u32[]{:S(2)}) copy-start(f32[28,4,8,128]{3,2,1,0:T(8,128)} %param.23) | copy-start | bytes 1376260
  29.6 16.2 %collective-permute-start = (f32[28,4,1,128]{3,2,1,0:T(1,128)}, f32[28,4,1,128]{3,2,1,0:T(1,128)S(1)}, u32[]{:S(2)}, u32[]{:S(2)}) collective-permute-start(f32[28,4,1,128]{3,2,1,0:T(1,128)} %copy.353), channel_id=1, source_target_pairs={{0,8},{8,16},{16,24},{24,32},{32,40},{40,48},{48,56},{56,64},{64,7... | collective-permute-start | bytes 172040 | tf_op jit(solution)/shard_map/ppermute | solution.py:15
  30.3 11.4 %collective-permute-start.1 = (f32[28,4,1,128]{3,2,1,0:T(1,128)}, f32[28,4,1,128]{3,2,1,0:T(1,128)S(1)}, u32[]{:S(2)}, u32[]{:S(2)}) collective-permute-start(f32[28,4,1,128]{3,2,1,0:T(1,128)} %copy.355), channel_id=1, source_target_pairs={{8,0},{16,8},{24,16},{32,24},{40,32},{48,40},{56,48},{64,56},{72,6... | collective-permute-start | bytes 172040 | tf_op jit(solution)/shard_map/ppermute | solution.py:18
  34.9 14.7 %collective-permute-start.4 = (f32[28,4,1,128]{3,2,1,0:T(1,128)}, f32[28,4,1,128]{3,2,1,0:T(1,128)S(1)}, u32[]{:S(2)}, u32[]{:S(2)}) collective-permute-start(f32[28,4,1,128]{3,2,1,0:T(1,128)} %get-tuple-element.556), channel_id=1, source_target_pairs={{8,0},{16,8},{24,16},{32,24},{40,32},{48,40},{56,48},{64,56},{72,6... | collective-permute-start | bytes 172040 | tf_op jit(solution)/shard_map/ppermute | solution.py:18
  34.9 27.9 %collective-permute-start.5 = (f32[28,4,1,128]{3,2,1,0:T(1,128)}, f32[28,4,1,128]{3,2,1,0:T(1,128)S(1)}, u32[]{:S(2)}, u32[]{:S(2)}) collective-permute-start(f32[28,4,1,128]{3,2,1,0:T(1,128)} %get-tuple-element.555), channel_id=1, source_target_pairs={{0,8},{8,16},{16,24},{24,32},{32,40},{40,48},{48,56},{56,64},{64,7... | collective-permute-start | bytes 172040 | tf_op jit(solution)/shard_map/ppermute | solution.py:15
  57.1 10.8 %collective-permute-start.2 = (f32[28,4,10,1]{0,2,3,1:T(8,128)}, f32[28,4,10,1]{0,2,3,1:T(8,128)}, u32[]{:S(2)}, u32[]{:S(2)}) collective-permute-start(f32[28,4,10,1]{0,2,3,1:T(8,128)} %copy.358), channel_id=1, source_target_pairs={{0,1},{1,2},{2,3},{3,4},{4,5},{5,6},{6,7},{7,0},{8,9},{9,10},{10,1... | collective-permute-start | bytes 13448 | tf_op jit(solution)/shard_map/ppermute | solution.py:15
  58.8 10.7 %collective-permute-start.3 = (f32[28,4,10,1]{0,2,3,1:T(8,128)}, f32[28,4,10,1]{0,2,3,1:T(8,128)}, u32[]{:S(2)}, u32[]{:S(2)}) collective-permute-start(f32[28,4,10,1]{0,2,3,1:T(8,128)} %copy.360), channel_id=1, source_target_pairs={{1,0},{2,1},{3,2},{4,3},{5,4},{6,5},{7,6},{0,7},{9,8},{10,9},{11,1... | collective-permute-start | bytes 13448 | tf_op jit(solution)/shard_map/ppermute | solution.py:18
  64.5 23.9 %collective-permute-start.6 = (f32[28,4,10,1]{0,2,3,1:T(8,128)}, f32[28,4,10,1]{0,2,3,1:T(8,128)}, u32[]{:S(2)}, u32[]{:S(2)}) collective-permute-start(f32[28,4,10,1]{0,2,3,1:T(8,128)} %copy.385), channel_id=1, source_target_pairs={{1,0},{2,1},{3,2},{4,3},{5,4},{6,5},{7,6},{0,7},{9,8},{10,9},{11,1... | collective-permute-start | bytes 13448 | tf_op jit(solution)/shard_map/ppermute | solution.py:18
  67.8 23.1 %collective-permute-start.7 = (f32[28,4,10,1]{0,2,3,1:T(8,128)}, f32[28,4,10,1]{0,2,3,1:T(8,128)}, u32[]{:S(2)}, u32[]{:S(2)}) collective-permute-start(f32[28,4,10,1]{0,2,3,1:T(8,128)} %copy.387), channel_id=1, source_target_pairs={{0,1},{1,2},{2,3},{3,4},{4,5},{5,6},{6,7},{7,0},{8,9},{9,10},{10,1... | collective-permute-start | bytes 13448 | tf_op jit(solution)/shard_map/ppermute | solution.py:15
  72.6 0.7 copy-start.35
  72.6 0.7 copy-start.63
  73.9 0.7 copy-start.37
  73.9 0.7 copy-start.47
  74.6 0.7 copy-start.38
  74.6 0.7 copy-start.48
  78.8 0.7 copy-start.46
  79.5 0.7 copy-start.45
  83.7 2.0 copy-start.28
  84.4 0.7 copy-start.29
  84.4 0.7 copy-start.55
  93.4 1.2 copy-start.2
  94.6 0.7 copy-start.62
  94.6 0.7 copy-start.36
  94.6 0.7 copy-start.44
  94.6 0.7 copy-start.27
  94.6 0.7 copy-start.33
  94.6 0.7 copy-start.53
  94.6 0.7 copy-start.61
  94.7 1.4 copy-start.1
  96.4 0.7 copy-start.22
  99.0 0.8 copy-start.25
  99.0 0.7 copy-start.26
  99.0 0.7 copy-start.52
  101.4 0.7 copy-start.19
  101.4 0.7 copy-start.40
  101.4 0.7 copy-start.70
  105.5 1.9 copy-start.60
  111.4 11.8 %copy-start.20 = (f32[3,4,8,128]{3,0,2,1:T(4,128)S(1)}, f32[3,4,8,128]{3,0,2,1:T(4,128)}, u32[]{:S(2)}) copy-start(f32[3,4,8,128]{3,0,2,1:T(4,128)} %get-tuple-element.576) | copy-start | bytes 147460
  123.3 0.7 copy-start.50
  123.3 0.7 copy-start.86
  (29 other events, 19.0 us)
